TPU v7x, 512 devices: a whole 4x8x8 slice. The times are simulated.
512 devices in a mesh: dp: 32 (over y, z_lo, core), seq: 16 (over x, z_hi).
Axes of the slice: x: 4, y: 8, z: 8 (z_hi: 4, z_lo: 2; z = z_hi * 2 + z_lo), core: 2. Of those that a mesh axis runs over, the one named last changes fastest.
Arguments:
- query_rows: bfloat16 [32, 2048, 2048], P('dp', 'seq'), may hold values from -6 to 6
- key_rows: bfloat16 [32, 2048, 2048], P('dp', 'seq'), may hold values from -0.5 to 0.5
- value_rows: bfloat16 [32, 2048, 2048], P('dp', 'seq'), may hold values from -6 to 6
- doc_starts: int32 [32, 2048], P('dp', 'seq'), may hold values 0 or 1
- decay_rates: int32 [16], replicated, may hold values from 1 to 100
- out_gain: float32 [2048], replicated, may hold values from 0.1 to 1.9
- cotangent: bfloat16 [32, 2048, 2048], P('dp', 'seq'), may hold values from -6 to 6
Outputs:
- normed: bfloat16 [32, 2048, 2048], P('dp', 'seq')
- grad_query: bfloat16 [32, 2048, 2048], P('dp', 'seq')
- grad_key: bfloat16 [32, 2048, 2048], P('dp', 'seq')
- grad_value: bfloat16 [32, 2048, 2048], P('dp', 'seq')
- grad_gain: float32 [2048], P('dp')
All inputs are finite; a program needn't handle non-finite values. No bound on the sum of `doc_starts` on one device may be relied on, other than what follows from the above.
Results may differ from a plain program's by a relative error of at most 0.00085.
Values may be sent and summed in bfloat16 or wider, within the bound.
No kernel may reach another device: no remote copies, remote signals or barrier semaphores. Data moves between devices by JAX's collectives and lax.ppermute only.
A program may use at most 64 MiB of HBM per device.

v0:
```python
import math
import jax
import jax.numpy as jnp
from jax import lax
from jax.sharding import PartitionSpec as P

E = 128
highest = lax.Precision.HIGHEST
epsilon = 1e-05


def prefix(part, axis, combine, identity, reverse):
    count = lax.axis_size(axis)
    place = lax.axis_index(axis)
    ahead = count - 1 - place if reverse else place
    gathered = jax.tree.map(lambda a: lax.all_gather(a, axis), part)
    state = jax.tree.map(lambda a, e: jnp.zeros_like(a) + jnp.asarray(e, a.dtype), part, identity)

    def one(hop, state):
        source = count - 1 - hop if reverse else hop
        return combine(
            state, jax.tree.map(lambda a: lax.dynamic_index_in_dim(a, source, 0, False), gathered)
        )

    return lax.fori_loop(0, ahead, one, state)


def block_terms(log_decay, marks):
    length = marks.shape[0]
    counted = jnp.cumsum(marks, dtype=jnp.int32)
    places = jnp.arange(length, dtype=jnp.float32)
    offsets = places[:, None] - places[None, :]
    inside = (counted[:, None] == counted[None, :]) & (offsets >= 0.0)
    weights = jnp.where(
        inside[None], jnp.exp2(log_decay[:, None, None] * jnp.maximum(offsets, 0.0)[None]), 0.0
    )
    fresh = (counted == 0).astype(jnp.float32)
    entry = fresh[:, None] * jnp.exp2(log_decay[None, :] * (places[:, None] + 1.0))
    latest = counted[length - 1]
    tail = jnp.where(
        (counted == latest)[:, None],
        jnp.exp2(log_decay[None, :] * (length - 1.0 - places)[:, None]),
        0.0,
    )
    through = (latest == 0).astype(jnp.float32) * jnp.exp2(log_decay * length)
    return (weights, entry, tail, through)


def state_sum(key_block, value_block, tail):
    return jnp.einsum("jhe,jhf->hef", key_block * tail[:, :, None], value_block, precision=highest)


def out_sum(query_block, key_block, value_block, state_in, weights, entry):
    scores = jnp.einsum("ihe,jhe->hij", query_block, key_block, precision=highest) * weights
    inner = jnp.einsum("hij,jhe->ihe", scores, value_block, precision=highest)
    carried = jnp.einsum("ihe,hef->ihf", query_block, state_in, precision=highest)
    return inner + entry[:, :, None] * carried


def run_chain(through, terms, start, backward):

    def advance(accum, item):
        factor, term = item
        return (factor[:, None, None] * accum + term, accum)

    return lax.scan(advance, start, (through, terms), reverse=backward)


def combine(earlier, later):
    return (earlier[0] * later[0], later[1] + later[0][:, None, None] * earlier[1])


def ahead_state(factor, state):
    result = prefix(
        (factor, state), "seq", combine, (jnp.ones_like(factor), jnp.zeros_like(state)), False
    )
    return result[1]


def behind_grad(factor, state):
    result = prefix(
        (factor, state), "seq", combine, (jnp.ones_like(factor), jnp.zeros_like(state)), True
    )
    return result[1]


def forward_local(query_seq, key_seq, value_seq, marks, log_decay, link):
    length, heads, width = query_seq.shape
    block = math.gcd(length, 512)
    count = length // block
    query_blocks = query_seq.astype(jnp.float32).reshape(count, block, heads, width)
    key_blocks = key_seq.astype(jnp.float32).reshape(count, block, heads, width)
    value_blocks = value_seq.astype(jnp.float32).reshape(count, block, heads, width)
    weights, entry, tail, through = jax.vmap(block_terms, (None, 0))(
        log_decay, marks.reshape(count, block)
    )

    def states_of(key_part, value_part):
        return jax.vmap(state_sum)(key_part, value_part, tail)

    states, state_back = jax.vjp(states_of, key_blocks, value_blocks)
    empty = jnp.zeros((heads, width, width), jnp.float32)
    own_state = run_chain(through, states, empty, False)[0]
    own_factor = jnp.prod(through, axis=0)
    device_in = link(own_factor, own_state)
    block_in = run_chain(through, states, device_in, False)[1]

    def outs_of(query_part, key_part, value_part, state_part):
        return jax.vmap(out_sum)(query_part, key_part, value_part, state_part, weights, entry)

    outs, out_back = jax.vjp(outs_of, query_blocks, key_blocks, value_blocks, block_in)
    saved = (through, own_factor, state_back, out_back, block, count)
    return (outs.reshape(length, heads * width), saved)


def backward_local(grad_rows, saved, link, heads, width):
    through, own_factor, state_back, out_back, block, count = saved
    length = grad_rows.shape[0]
    grad_blocks = grad_rows.reshape(count, block, heads, width)
    grad_q_part, grad_k_part, grad_v_part, grad_state = out_back(grad_blocks)
    empty = jnp.zeros((heads, width, width), jnp.float32)
    own_grad = run_chain(through, grad_state, empty, True)[0]
    device_out = link(own_factor, own_grad)
    block_out = run_chain(through, grad_state, device_out, True)[1]
    extra_key, extra_value = state_back(block_out)
    flat = (length, heads * width)
    return (
        grad_q_part.reshape(flat),
        (grad_k_part + extra_key).reshape(flat),
        (grad_v_part + extra_value).reshape(flat),
    )


def normalize(mixed, out_gain, cotangent):

    def apply(attn, gain_vec):
        scale = lax.rsqrt(jnp.mean(attn * attn, axis=-1, keepdims=True) + epsilon)
        return attn * scale * gain_vec

    result, back = jax.vjp(apply, mixed, out_gain)
    grad_out, gain_part = back(cotangent.astype(jnp.float32))
    return (result.astype(jnp.bfloat16), grad_out, gain_part)


def per_device(query_rows, key_rows, value_rows, doc_starts, decay_rates, out_gain, cotangent):
    local_tokens = query_rows.shape[1]
    total = local_tokens * lax.axis_size("seq")
    log_decay = -decay_rates.astype(jnp.float32) / total
    heads = query_rows.shape[2] // E
    shaped = (local_tokens, heads, E)
    outs, saved = forward_local(
        query_rows[0].reshape(shaped),
        key_rows[0].reshape(shaped),
        value_rows[0].reshape(shaped),
        doc_starts[0],
        log_decay,
        ahead_state,
    )
    normed, grad_out, gain_part = normalize(outs[None], out_gain, cotangent)
    grads = backward_local(grad_out[0], saved, behind_grad, heads, E)
    grad_query = grads[0][None].astype(jnp.bfloat16)
    grad_key = grads[1][None].astype(jnp.bfloat16)
    grad_value = grads[2][None].astype(jnp.bfloat16)
    summed = lax.psum(gain_part, "seq")
    grad_gain = lax.psum_scatter(summed, "dp", scatter_dimension=0, tiled=True)
    return (normed, grad_query, grad_key, grad_value, grad_gain)


def solution(mesh):
    return jax.shard_map(
        per_device,
        mesh=mesh,
        in_specs=(
            P("dp", "seq", None),
            P("dp", "seq", None),
            P("dp", "seq", None),
            P("dp", "seq"),
            P(),
            P(),
            P("dp", "seq", None),
        ),
        out_specs=(
            P("dp", "seq", None),
            P("dp", "seq", None),
            P("dp", "seq", None),
            P("dp", "seq", None),
            P("dp"),
        ),
        check_vma=False,
    )
```

profile of v0, /device:TPU:1, one launch (start us, length us, event | category | flops | bytes accessed | tf_op | source)
XLA Modules:
  0.0 518.3 jit_solution(9662311050770830135)
XLA Ops:
  7.2 0.0 all-gather.7.cloned.1.call-start
  7.2 1.0 reduce_window_sum.11
  8.2 0.6 slice.3
  9.4 0.7 compare_convert_fusion
  10.1 1.1 copy.63
  11.2 0.0 copy-start.3
  11.3 1.2 copy.64
  12.4 1.3 dynamic-slice.3
  14.4 0.8 fusion.39
  15.1 0.1 exponential_multiply_fusion
  15.2 2.3 convolution_add_fusion.2
  17.5 0.0 all-gather.7.cloned.1.call-update
  17.6 0.0 all-gather.5.cloned.1.call-start
  17.6 46.0 %all-reduce = f32[256]{0:T(256)S(1)} all-reduce(f32[256]{0:T(256)S(1)} %get-tuple-element.232), channel_id=3, replica_groups=mesh['dp'=32,'seq'=16] {'seq'}, use_global_device_ids=true, to_apply=%add | all-reduce | flops 256 | bytes 2048
  63.6 0.1 reshape.542
  63.7 1.2 copy.62
  64.9 0.0 copy-start.2
  64.9 0.1 fusion.36
  65.0 1.5 convolution_multiply_fusion.1
  66.5 165.6 %all-gather.7.cloned.1.call-done = f32[256,128,128]{2,1,0:T(8,128)} async-done(((f32[16,128,128]{2,1,0:T(8,128)}), f32[256,128,128]{2,1,0:T(8,128)}) %all-gather.7.cloned.1.call-update) | async-done | bytes 16777232 | tf_op jit(solution)/shard_map/all_gather | solution.py:16
  232.1 0.1 broadcast_in_dim.43.clone
  232.3 1.0 fusion.1
  233.3 3.4 multiply_reduce_fusion
  236.7 0.0 copy-done.2
  236.7 1.6 copy.43
  238.3 1.4 fusion.12
  239.7 2.7 add_add_fusion
  242.4 1.5 copy.46
  243.9 2.7 fusion.4
  246.7 2.5 copy.52
  249.2 0.0 all-gather.5.cloned.1.call-update
  249.2 1.3 dynamic-slice.4
  251.1 1.2 convolution_multiply_fusion
  252.4 1.1 fusion.14
  253.5 1.2 fusion.7
  254.7 1.0 copy.55
  255.7 55.1 %all-reduce.1 = f32[2048]{0:T(1024)S(1)} all-reduce(f32[2048]{0:T(1024)S(1)} %get-tuple-element.204), channel_id=4, replica_groups=mesh['dp'=32,'seq'=16] {'dp'}, use_global_device_ids=true, to_apply=%region_9.10.clone | all-reduce | flops 2048 | bytes 16384
  310.8 0.1 dynamic-slice.5
  310.9 66.8 %psum.8 = f32[64]{0:T(128)} all-reduce(f32[64]{0:T(128)S(1)} %dynamic-slice.5), channel_id=1, replica_groups=mesh['dp'=32,'seq'=16] {'seq'}, use_global_device_ids=true, to_apply=%region_8.9 | all-reduce | flops 64 | bytes 512 | tf_op jit(solution)/shard_map/psum | solution.py:164
  377.7 3.4 fusion.40
  381.2 99.2 %all-gather.5.cloned.1.call-done = f32[16,16,128,128]{3,2,1,0:T(8,128)} async-done(((f32[1,16,128,128]{3,2,1,0:T(8,128)}), f32[16,16,128,128]{3,2,1,0:T(8,128)}) %all-gather.5.cloned.1.call-update) | async-done | bytes 16777232 | tf_op jit(solution)/shard_map/all_gather | solution.py:16
  480.4 0.1 broadcast_in_dim.43
  480.5 22.4 %while.17 = (s32[]{:T(128)}, f32[16,128,128]{2,1,0:T(8,128)S(1)}, s32[]{:T(128)}, f32[16,16,128,128]{3,2,1,0:T(8,128)}, f32[16,16]{1,0:T(8,128)S(1)}, /*index=5*/s32[]{:T(128)}, s32[]{:T(128)}, s32[]{:T(128)}, s32[]{:T(128)}) while((s32[]{:T(128)}, f32[16,128,128]{2,1,0:T(8,128)S(1)}, s32[]{:T(128)}, f32[16,16,128,128]{3,2,1,0:T(8,128)}, ...), condition=%wide.region_6.7_spmd, body=%wide.region_5.6_spmd.sunk | while | flops 524294 | bytes 3146075 | solution.py:25
  480.5 1.4 bitcast_add_fusion.5
  482.0 1.4 bitcast_add_fusion.5
  483.5 1.4 bitcast_add_fusion.5
  485.0 1.4 bitcast_add_fusion.5
  486.5 1.4 bitcast_add_fusion.5
  488.0 1.4 bitcast_add_fusion.5
  489.5 1.4 bitcast_add_fusion.5
  491.0 1.4 bitcast_add_fusion.5
  492.5 1.4 bitcast_add_fusion.5
  494.0 1.4 bitcast_add_fusion.5
  495.4 1.4 bitcast_add_fusion.5
  496.9 1.4 bitcast_add_fusion.5
  498.4 1.4 bitcast_add_fusion.5
  499.9 1.4 bitcast_add_fusion.5
  501.4 1.4 bitcast_add_fusion.5
  502.9 1.2 fusion.5
  504.1 3.5 fusion.8
  507.6 0.0 copy-done.1
  507.6 1.8 fusion.6
  509.5 1.0 copy.56
  510.5 1.0 copy.57
  (25 shorter events, 0.2 us)
Async XLA Ops:
  7.2 225.0 %all-gather.7.cloned.1.call-start = ((), (), s32[]{:S(2)}) async-start(), calls=%async_computation.1 | async-start | bytes 17825792 | tf_op jit(solution)/shard_map/all_gather | solution.py:16
  11.2 227.0 %copy-start.3 = (f32[2048]{0:T(1024)S(1)}, f32[2048]{0:T(1024)}, u32[]{:S(2)}) copy-start(f32[2048]{0:T(1024)} %param.16) | copy-start | bytes 24580
  17.6 462.8 %all-gather.5.cloned.1.call-start = ((), (), s32[]{:S(2)}) async-start(), calls=%async_computation | async-start | bytes 17825792 | tf_op jit(solution)/shard_map/all_gather | solution.py:16
  64.9 171.8 %copy-start.2 = (bf16[16,8,16,128]{3,2,1,0:T(8,128)(2,1)}, bf16[16,8,16,128]{3,2,1,0:T(8,128)(2,1)S(1)}, u32[]{:S(2)}) copy-start(bf16[16,8,16,128]{3,2,1,0:T(8,128)(2,1)S(1)} %copy.62) | copy-start | bytes 1572868
  252.4 1.1 copy-start
  381.2 126.4 %copy-start.1 = (f32[16,128,128]{2,1,0:T(8,128)S(1)}, f32[16,128,128]{2,1,0:T(8,128)}, u32[]{:S(2)}) copy-start(f32[16,128,128]{2,1,0:T(8,128)} %copy-done) | copy-start | bytes 3145732
Sparse Core Ops, SparseCore 0:
  17.7 214.4 all-gather.6
  249.3 230.9 all-gather.4
where the time goes:
time: 520 us; the launch traced here: 518 us
  waiting for transfers between devices  265 us (51%)
  blocking collectives  168 us (32%)
  other arithmetic  28.4 us (5%)
  matrix products  24.6 us (5%)
  between operations  16.2 us (3%)
  local copies, waits for them, and re-layouts  15.8 us (3%)
    all_gather x2, waiting for transfers between devices, prefix(): gathered = jax.tree.map(lambda a: lax.all_gather(a, axis), part)  265 us
    unnamed x2, blocking collectives  101 us
    psum x1, blocking collectives, per_device(): summed = lax.psum(gain_part, 'seq')  66.8 us
    add x15, other arithmetic, combine(): later[1] + later[0][:, None, None] * earlier[1]  21.7 us
  transfers between devices with their start and end apart: 2, of which 2 were waited for; matrix products, arithmetic and copies ran while one was open for 2% of the time, Pallas kernels for 0%

commit v1 on v0

--- a/solution.py
+++ b/solution.py
@@ -161,7 +161,7 @@
     grad_query = grads[0][None].astype(jnp.bfloat16)
     grad_key = grads[1][None].astype(jnp.bfloat16)
     grad_value = grads[2][None].astype(jnp.bfloat16)
-    summed = lax.psum(gain_part, "seq")
+    summed = jnp.sum(lax.all_gather(gain_part, "seq"), axis=0)
     grad_gain = lax.psum_scatter(summed, "dp", scatter_dimension=0, tiled=True)
     return (normed, grad_query, grad_key, grad_value, grad_gain)
 

time: 520 us -> 519 us (level)
  waiting for transfers between devices: 265 us -> 247 us
  blocking collectives: 168 us -> 185 us
    psum x1 -> x0, blocking collectives: 66.8 us -> none  [per_device(): summed = lax.psum(gain_part, 'seq')]
    all_gather x0 -> x1, blocking collectives: none -> 62.8 us  [per_device(): summed = jnp.sum(lax.all_gather(gain_part, 'seq'), axis=0)]
    unnamed x2, blocking collectives: 101 us -> 122 us
    all_gather x2, waiting for transfers between devices: 265 us -> 247 us  [prefix(): gathered = jax.tree.map(lambda a: lax.all_gather(a, axis), part)]
where the time goes in v1:
time: 519 us; the launch traced here: 518 us
  waiting for transfers between devices  247 us (48%)
  blocking collectives  185 us (36%)
  other arithmetic  28.4 us (5%)
  matrix products  24.5 us (5%)
  local copies, waits for them, and re-layouts  16.3 us (3%)
  between operations  16.2 us (3%)
    all_gather x2, waiting for transfers between devices, prefix(): gathered = jax.tree.map(lambda a: lax.all_gather(a, axis), part)  247 us
    unnamed x2, blocking collectives  122 us
    all_gather x1, blocking collectives, per_device(): summed = jnp.sum(lax.all_gather(gain_part, 'seq'), axis=0)  62.8 us
    add x15, other arithmetic, combine(): later[1] + later[0][:, None, None] * earlier[1]  21.7 us
  transfers between devices with their start and end apart: 2, of which 2 were waited for; matrix products, arithmetic and copies ran while one was open for 2% of the time, Pallas kernels for 0%

profile of v1, /device:TPU:1, one launch (start us, length us, event | category | flops | bytes accessed | tf_op | source)
XLA Modules:
  0.0 517.7 jit_solution(2409550529102110548)
XLA Ops:
  7.2 0.0 all-gather.8.cloned.1.call-start
  7.2 1.0 reduce_window_sum.11
  8.2 0.6 slice.3
  9.4 0.7 compare_convert_fusion
  10.1 1.1 copy.86
  11.2 0.0 copy-start.3
  11.3 1.2 copy.87
  12.4 1.3 dynamic-slice.3
  14.4 0.8 fusion.39
  15.1 0.1 exponential_multiply_fusion
  15.2 2.3 convolution_add_fusion.2
  17.5 0.0 all-gather.8.cloned.1.call-update
  17.6 0.0 all-gather.6.cloned.1.call-start
  17.6 46.0 %all-reduce = f32[256]{0:T(256)S(1)} all-reduce(f32[256]{0:T(256)S(1)} %get-tuple-element.237), channel_id=3, replica_groups=mesh['dp'=32,'seq'=16] {'seq'}, use_global_device_ids=true, to_apply=%add | all-reduce | flops 256 | bytes 2048
  63.6 0.1 reshape.543
  63.7 1.2 copy.85
  64.9 0.0 copy-start.2
  64.9 0.1 fusion.36
  65.0 1.5 convolution_multiply_fusion.1
  66.5 165.6 %all-gather.8.cloned.1.call-done = f32[256,128,128]{2,1,0:T(8,128)} async-done(((f32[16,128,128]{2,1,0:T(8,128)}), f32[256,128,128]{2,1,0:T(8,128)}) %all-gather.8.cloned.1.call-update) | async-done | bytes 16777232 | tf_op jit(solution)/shard_map/all_gather | solution.py:16
  232.1 0.1 broadcast_in_dim.43.clone
  232.3 1.0 fusion.1
  233.3 3.4 multiply_reduce_fusion
  236.7 0.0 copy-done.2
  236.7 1.6 copy.66
  238.3 1.4 fusion.12
  239.7 2.7 add_add_fusion
  242.4 1.5 copy.69
  243.9 2.7 fusion.4
  246.7 2.5 copy.75
  249.2 0.0 all-gather.6.cloned.1.call-update
  249.2 1.3 dynamic-slice.4
  251.1 62.8 %all-gather.2 = f32[32768]{0:T(1024)S(1)} all-gather(f32[2048]{0:T(1024)S(1)} %get-tuple-element.209), channel_id=4, replica_groups=mesh['dp'=32,'seq'=16] {'seq'}, dimensions={0}, use_global_device_ids=true | all-gather | bytes 139264 | tf_op jit(solution)/shard_map/all_gather | solution.py:164
  314.0 1.2 convolution_multiply_fusion
  315.2 0.0 copy-start
  315.2 1.1 fusion.14
  316.3 1.2 fusion.7
  317.5 1.0 copy.78
  318.6 76.2 %all-reduce.1 = f32[2048]{0:T(1024)S(1)} all-reduce(f32[2048]{0:T(1024)S(1)} %reduce_sum.41), channel_id=5, replica_groups=mesh['dp'=32,'seq'=16] {'dp'}, use_global_device_ids=true, to_apply=%region_9.10.clone | all-reduce | flops 2048 | bytes 16384
  394.8 0.6 dynamic-slice.5
  395.4 3.4 fusion.40
  398.8 81.0 %all-gather.6.cloned.1.call-done = f32[16,16,128,128]{3,2,1,0:T(8,128)} async-done(((f32[1,16,128,128]{3,2,1,0:T(8,128)}), f32[16,16,128,128]{3,2,1,0:T(8,128)}) %all-gather.6.cloned.1.call-update) | async-done | bytes 16777232 | tf_op jit(solution)/shard_map/all_gather | solution.py:16
  479.8 0.1 broadcast_in_dim.43
  479.9 22.4 %while.17 = (s32[]{:T(128)}, f32[16,128,128]{2,1,0:T(8,128)S(1)}, s32[]{:T(128)}, f32[16,16,128,128]{3,2,1,0:T(8,128)}, f32[16,16]{1,0:T(8,128)S(1)}, /*index=5*/s32[]{:T(128)}, s32[]{:T(128)}, s32[]{:T(128)}, s32[]{:T(128)}) while((s32[]{:T(128)}, f32[16,128,128]{2,1,0:T(8,128)S(1)}, s32[]{:T(128)}, f32[16,16,128,128]{3,2,1,0:T(8,128)}, ...), condition=%wide.region_6.7_spmd, body=%wide.region_5.6_spmd.sunk | while | flops 524294 | bytes 3146075 | solution.py:25
  479.9 1.4 bitcast_add_fusion.5
  481.4 1.4 bitcast_add_fusion.5
  482.9 1.4 bitcast_add_fusion.5
  484.4 1.4 bitcast_add_fusion.5
  485.9 1.4 bitcast_add_fusion.5
  487.4 1.4 bitcast_add_fusion.5
  488.9 1.4 bitcast_add_fusion.5
  490.3 1.4 bitcast_add_fusion.5
  491.8 1.4 bitcast_add_fusion.5
  493.3 1.4 bitcast_add_fusion.5
  494.8 1.4 bitcast_add_fusion.5
  496.3 1.4 bitcast_add_fusion.5
  497.8 1.4 bitcast_add_fusion.5
  499.3 1.4 bitcast_add_fusion.5
  500.8 1.4 bitcast_add_fusion.5
  502.3 1.2 fusion.5
  503.5 3.5 fusion.8
  507.0 1.8 fusion.6
  508.9 1.0 copy.79
  509.9 1.0 copy.80
  (27 shorter events, 0.3 us)
Async XLA Ops:
  7.2 225.0 %all-gather.8.cloned.1.call-start = ((), (), s32[]{:S(2)}) async-start(), calls=%async_computation.1 | async-start | bytes 17825792 | tf_op jit(solution)/shard_map/all_gather | solution.py:16
  11.2 227.0 %copy-start.3 = (f32[2048]{0:T(1024)S(1)}, f32[2048]{0:T(1024)}, u32[]{:S(2)}) copy-start(f32[2048]{0:T(1024)} %param.16) | copy-start | bytes 24580
  17.6 462.2 %all-gather.6.cloned.1.call-start = ((), (), s32[]{:S(2)}) async-start(), calls=%async_computation | async-start | bytes 17825792 | tf_op jit(solution)/shard_map/all_gather | solution.py:16
  64.9 171.8 %copy-start.2 = (bf16[16,8,16,128]{3,2,1,0:T(8,128)(2,1)}, bf16[16,8,16,128]{3,2,1,0:T(8,128)(2,1)S(1)}, u32[]{:S(2)}) copy-start(bf16[16,8,16,128]{3,2,1,0:T(8,128)(2,1)S(1)} %copy.85) | copy-start | bytes 1572868
  315.2 1.1 copy-start
  398.8 108.2 %copy-start.1 = (f32[16,128,128]{2,1,0:T(8,128)S(1)}, f32[16,128,128]{2,1,0:T(8,128)}, u32[]{:S(2)}) copy-start(f32[16,128,128]{2,1,0:T(8,128)} %copy-done) | copy-start | bytes 3145732
Sparse Core Ops, SparseCore 0:
  17.7 214.4 all-gather.7
  249.3 230.3 all-gather.5
